TPU v7x, 256 devices: a whole 4x4x8 slice. The times are simulated.
256 devices in a mesh: slab: 32 (over z, x), coil: 8 (over y, core).
Axes of the slice: x: 4, y: 4, z: 8, core: 2. Of those that a mesh axis runs over, the one named last changes fastest.
Arguments:
- noisy: float32 [2, 64, 256, 128], P(None, 'slab', 'coil'), may hold values from -6 to 6
- step_index: int32 [], replicated, may hold values from 200 to 599
- w_in: bfloat16 [3, 3, 3, 32, 2], replicated, may hold values from -0.875 to 0.875
- w_mid: bfloat16 [3, 3, 3, 32, 32], replicated, may hold values from -0.21875 to 0.21875
- w_out: bfloat16 [3, 3, 3, 2, 32], replicated, may hold values from -0.21875 to 0.21875
- time_weight: float32 [32, 32], replicated, may hold values from -1 to 1
- sens: float32 [16, 2, 64, 256, 128], P('coil', None, 'slab')
- kdata: float32 [16, 2, 64, 256, 128], P('coil', None, None, 'slab'), may hold values from -4 to 4
- mask: int32 [64, 256], P(None, 'slab'), may hold values from 0 to 1, as said below
Outputs:
- recon: float32 [2, 64, 256, 128], P(None, 'slab', 'coil')
- next_sample: float32 [2, 64, 256, 128], P(None, 'slab', 'coil')
Inputs may be any that keep to these rules, and one draw needn't show every extreme that they name: mask[kz, ky] is 1 wherever min(kz, 64 - kz) < max(1, 4) and min(ky, 256 - ky) < max(1, 8); every other entry is 1 with chance one in three.
All inputs are finite; a program needn't handle non-finite values.
Results may differ from a plain program's by a relative error of at most 0.0023.
Values may be sent and summed in bfloat16 or wider, within the bound.
No kernel may reach another device: no remote copies, remote signals or barrier semaphores. Data moves between devices by JAX's collectives and lax.ppermute only.
A program may use at most 64 MiB of HBM per device.

v0:
```python
import math
import jax
import jax.numpy as jnp
from jax import lax
from jax.sharding import PartitionSpec as P

ITERS = 2
STEPS = 1000
STRIDE = 20
REG_WEIGHT = 0.5
HIGHEST_PRECISION = lax.Precision.HIGHEST


def extended(cells, sides, width):
    for axis, dim in sides:
        count = lax.axis_size(axis)
        ends = count - 1
        head = lax.slice_in_dim(cells, 0, width, axis=dim)
        tail = lax.slice_in_dim(cells, cells.shape[dim] - width, cells.shape[dim], axis=dim)
        cells = jnp.concatenate(
            [
                lax.ppermute(tail, axis, [(i, (i + 1) % count) for i in range(ends)]),
                cells,
                lax.ppermute(head, axis, [((i + 1) % count, i) for i in range(ends)]),
            ],
            axis=dim,
        )
    return cells


def plan_level(step_value):
    angle = (step_value / STEPS + 0.008) / 1.008 * (math.pi / 2)
    return jnp.cos(angle) ** 2


def time_bias(step_value, time_weight):
    half = time_weight.shape[0] // 2
    freqs = jnp.exp(-math.log(10000.0) * jnp.arange(half, dtype=jnp.float32) / half)
    phase = step_value * freqs
    embed = jnp.concatenate([jnp.sin(phase), jnp.cos(phase)])
    return jnp.dot(embed, time_weight, precision=HIGHEST_PRECISION)


def conv_layer(inputs, weights):
    padded = extended(inputs, (("slab", 1), ("coil", 2)), 1)
    kernel = jnp.transpose(weights, (3, 4, 0, 1, 2))
    result = lax.conv_general_dilated(
        padded[None],
        kernel,
        (1, 1, 1),
        ((0, 0), (0, 0), (1, 1)),
        dimension_numbers=("NCDHW", "OIDHW", "NCDHW"),
        preferred_element_type=jnp.float32,
    )
    return result[0]


def dft_blocks(length, inverse):
    index = jnp.arange(length, dtype=jnp.int32)
    product = index[:, None] * index[None, :] % length
    theta = product.astype(jnp.float32) * (2.0 * math.pi / length)
    cosine = jnp.cos(theta) / math.sqrt(length)
    sine = jnp.sin(theta) / math.sqrt(length)
    if inverse:
        sine = -sine
    upper = jnp.stack([cosine, sine], axis=1)
    lower = jnp.stack([-sine, cosine], axis=1)
    return jnp.stack([upper, lower], axis=0)


def along_last(data, blocks):
    return jnp.einsum("pkqn,cqzyn->cpzyk", blocks, data, precision=HIGHEST_PRECISION)


def along_rows(data, blocks):
    return jnp.einsum("pkqn,cqzny->cpzky", blocks, data, precision=HIGHEST_PRECISION)


def along_depth(data, blocks):
    return jnp.einsum("pkqn,cqnyx->cpkyx", blocks, data, precision=HIGHEST_PRECISION)


def times_sens(sens, image):
    real_part = sens[:, 0] * image[0] - sens[:, 1] * image[1]
    imag_part = sens[:, 0] * image[1] + sens[:, 1] * image[0]
    return jnp.stack([real_part, imag_part], axis=1)


def times_conj(sens, images):
    real_part = jnp.sum(sens[:, 0] * images[:, 0] + sens[:, 1] * images[:, 1], axis=0)
    imag_part = jnp.sum(sens[:, 0] * images[:, 1] - sens[:, 1] * images[:, 0], axis=0)
    return jnp.stack([real_part, imag_part])


def coil_term(image_full, sens, kdata_x, weight, blocks, with_data):
    forward_y, forward_z, inverse_y, inverse_z = blocks
    coil_images = times_sens(sens, image_full)
    spectrum = along_rows(coil_images, forward_y)
    pencils = lax.all_to_all(
        spectrum.astype(jnp.bfloat16), "slab", split_axis=3, concat_axis=2, tiled=True
    ).astype(jnp.float32)
    kspace = along_depth(pencils, forward_z)
    if with_data:
        kspace = weight * (kdata_x - kspace)
    else:
        kspace = weight * kspace
    back = along_depth(kspace, inverse_z)
    slabs = lax.all_to_all(
        back.astype(jnp.bfloat16), "slab", split_axis=2, concat_axis=3, tiled=True
    ).astype(jnp.float32)
    images = along_rows(slabs, inverse_y)
    return times_conj(sens, images)


def combine_coils(partial_value):
    count = lax.axis_size("coil")
    pieces = lax.all_to_all(partial_value, "coil", split_axis=2, concat_axis=0, tiled=True)
    pieces = pieces.reshape((count, partial_value.shape[0]) + pieces.shape[1:])
    return jnp.sum(pieces, axis=0)


def gather_rows(value):
    return lax.all_gather(value, "coil", axis=2, tiled=True)


def global_sums(values):
    axes = ("slab", "coil")
    count = lax.axis_size("slab") * lax.axis_size("coil")
    spread = jnp.broadcast_to(values[None], (count,) + values.shape)
    return jnp.sum(lax.all_to_all(spread, axes, split_axis=0, concat_axis=0, tiled=True), axis=0)


def body(noisy, step_index, w_in, w_mid, w_out, time_weight, sens, kdata, mask):
    step_value = step_index.astype(jnp.float32)
    signal_level = plan_level(step_value)
    prior_level = plan_level(step_value - STRIDE)
    bias = time_bias(step_value, time_weight)
    hidden = jax.nn.silu(
        conv_layer(noisy.astype(jnp.bfloat16), w_in) + bias[:, None, None, None]
    ).astype(jnp.bfloat16)
    mixed = (hidden.astype(jnp.float32) + jax.nn.silu(conv_layer(hidden, w_mid))).astype(
        jnp.bfloat16
    )
    noise_pred = conv_layer(mixed, w_out)
    estimate = (noisy - jnp.sqrt(1.0 - signal_level) * noise_pred) / jnp.sqrt(signal_level)
    depth_full = kdata.shape[2]
    rows_full = sens.shape[3]
    width = sens.shape[4]
    blocks = (
        dft_blocks(rows_full, False),
        dft_blocks(depth_full, False),
        dft_blocks(rows_full, True),
        dft_blocks(depth_full, True),
    )
    kdata_x = along_last(kdata, dft_blocks(width, True))
    weight = mask.astype(jnp.float32)[None, None, :, :, None]

    def operator(image, with_data):
        return combine_coils(
            coil_term(gather_rows(image), sens, kdata_x, weight, blocks, with_data)
        )

    solution = estimate
    residual = operator(estimate, True)
    direction = residual
    norm_now = None
    for iteration in range(ITERS):
        final_turn = iteration + 1 == ITERS
        image = operator(direction, False) + REG_WEIGHT * direction
        if norm_now is None:
            sums = global_sums(
                jnp.stack([jnp.sum(residual * residual), jnp.sum(direction * image)])
            )
            norm_now, curvature = (sums[0], sums[1])
        else:
            curvature = global_sums(jnp.stack([jnp.sum(direction * image)]))[0]
        step_size = norm_now / curvature
        solution = solution + step_size * direction
        if not final_turn:
            residual = residual - step_size * image
            norm_next = global_sums(jnp.stack([jnp.sum(residual * residual)]))[0]
            direction = residual + norm_next / norm_now * direction
            norm_now = norm_next
    recon = solution
    next_sample = jnp.sqrt(prior_level) * recon + jnp.sqrt(1.0 - prior_level) * noise_pred
    return (recon, next_sample)


def solution(mesh):
    return jax.shard_map(
        body,
        mesh=mesh,
        in_specs=(
            P(None, "slab", "coil", None),
            P(),
            P(),
            P(),
            P(),
            P(),
            P("coil", None, "slab", None, None),
            P("coil", None, None, "slab", None),
            P(None, "slab"),
        ),
        out_specs=(P(None, "slab", "coil", None), P(None, "slab", "coil", None)),
        check_vma=False,
    )
```

profile of v0, /device:TPU:1, one launch (start us, length us, event | category | flops | bytes accessed | tf_op | source)
XLA Modules:
  0.0 684.9 jit_solution(6342718819612224770)
XLA Ops:
  22.7 7.8 %broadcast_select_fusion.1 = f32[2,32,8,17,32]{4,2,3,1,0:T(8,128)S(1)} fusion(pred[8,17]{0,1:T(8,128)(4,1)} %constant.113, bf16[3,3,3,32,2]{3,4,2,1,0:T(2,128)(2,1)} %param.11, bf16[2,4,34,1,7,2]{4,0,5,2,1,3:T(2,128)(2,1)S(1)} %slice.155, bf16[2,4,34,1,8,17]{4,0,5,2,1,3:T(2,128)(2,1)S(1)} %copy.378), kind=kOutput, calls=%fused_computation.23 | convolution fusion | flops 30607616 | bytes 1199304 | tf_op jit(solution)/shard_map/conv_general_dilated | solution.py:47
  75.3 8.1 %copy.497 = bf16[32,4,34,1,128]{2,0,4,1,3:T(8,128)(2,1)} copy(bf16[32,4,34,1,128]{0,2,4,1,3:T(8,128)(2,1)} %maximum_bitcast_fusion) | data formatting | bytes 2228224
  88.5 8.7 %copy.386 = bf16[32,4,34,1,8,17]{0,4,5,2,1,3:T(8,128)(2,1)} copy(bf16[32,4,34,1,8,17]{2,0,5,4,1,3:T(8,128)(2,1)} %bitcast.328) | data formatting | bytes 2367488 | tf_op jit(solution)/shard_map/conv_general_dilated | solution.py:47
  98.5 8.6 %broadcast_select_fusion = f32[2,32,8,17,32]{4,2,3,1,0:T(8,128)S(1)} fusion(pred[8,17]{0,1:T(8,128)(4,1)S(1)} %copy-done.25, bf16[3,3,3,32,32]{4,3,2,1,0:T(8,128)(2,1)S(1)} %copy-done.26, bf16[32,4,34,1,7,2]{0,4,5,2,1,3:T(8,128)(2,1)S(1)} %slice.159, bf16[32,4,34,1,8,17]{0,4,5,2,1,3:T(8,128)(2,1)} %copy.386), kind=kOutput, calls=%fused_computation.22 | convolution fusion | flops 485543936 | bytes 2475144 | tf_op jit(solution)/shard_map/conv_general_dilated | solution.py:47
  156.4 8.1 %copy.498 = bf16[32,4,34,1,128]{2,0,4,1,3:T(8,128)(2,1)} copy(bf16[32,4,34,1,128]{0,2,4,1,3:T(8,128)(2,1)} %maximum_bitcast_fusion.1) | data formatting | bytes 2228224
  169.6 8.7 %copy.394 = bf16[32,4,34,1,8,17]{0,4,5,2,1,3:T(8,128)(2,1)} copy(bf16[32,4,34,1,8,17]{2,0,5,4,1,3:T(8,128)(2,1)} %bitcast.327) | data formatting | bytes 2367488 | tf_op jit(solution)/shard_map/conv_general_dilated | solution.py:47
  179.5 139.8 %fusion.11 = f32[2,32,8,17,2]{2,4,3,1,0:T(2,128)} fusion(bf16[3,3,3,2,32]{4,3,2,1,0:T(2,128)(2,1)S(1)} %copy-done.27, bf16[32,4,34,1,7,2]{0,4,5,2,1,3:T(8,128)(2,1)S(1)} %slice.163, bf16[32,4,34,1,8,17]{0,4,5,2,1,3:T(8,128)(2,1)} %copy.394), kind=kOutput, calls=%fused_computation.11 | convolution fusion | flops 34050048 | bytes 1378688 | tf_op jit(solution)/shard_map/conv_general_dilated | solution.py:47
  325.5 14.1 %all_gather.9 = f32[2,2,256,128]{3,1,0,2:T(2,128)S(1)} all-gather(f32[2,2,32,128]{3,1,0,2:T(2,128)S(1)} %fusion.74), channel_id=1, replica_groups=mesh['slab'=32,'coil'=8] {'coil'}, dimensions={2}, use_global_device_ids=true | all-gather | bytes 589824 | tf_op jit(solution)/shard_map/all_gather | solution.py:123
  350.0 14.7 %all-to-all-start = ((bf16[2,2,2,256,128]{4,1,2,0,3:T(2,128)(2,1)}), bf16[2,2,2,256,128]{4,1,2,0,3:T(2,128)(2,1)S(1)}, u32[]{:S(2)}, u32[]{:S(2)}) async-start(bf16[2,2,2,256,128]{4,1,2,0,3:T(2,128)(2,1)} %copy.404), calls=%async_computation | async-start | bytes 1048576 | tf_op jit(solution)/shard_map/all_to_all | solution.py:99
  369.0 12.5 %all-to-all-done = bf16[2,2,2,256,128]{4,1,2,0,3:T(2,128)(2,1)S(1)} async-done(((bf16[2,2,2,256,128]{4,1,2,0,3:T(2,128)(2,1)}), bf16[2,2,2,256,128]{4,1,2,0,3:T(2,128)(2,1)S(1)}, u32[]{:S(2)}, u32[]{:S(2)}) %all-to-all-start) | async-done | bytes 524320 | tf_op jit(solution)/shard_map/all_to_all | solution.py:99
  385.3 20.3 %all_to_all.162 = bf16[2,2,64,8,128]{4,1,3,0,2:T(2,128)(2,1)S(1)} all-to-all(bf16[2,2,64,8,128]{4,1,3,0,2:T(2,128)(2,1)S(1)} %copy.408), channel_id=1, replica_groups=mesh['slab'=32,'coil'=8] {'slab'}, dimensions={2} | all-to-all | bytes 1048576 | tf_op jit(solution)/shard_map/all_to_all | solution.py:108
  410.0 16.8 %all_to_all.163 = f32[2,2,256,128]{3,1,0,2:T(2,128)} all-to-all(f32[2,2,256,128]{3,1,0,2:T(2,128)} %copy.412), channel_id=1, replica_groups=mesh['slab'=32,'coil'=8] {'coil'}, dimensions={2} | all-to-all | bytes 1048576 | tf_op jit(solution)/shard_map/all_to_all | solution.py:117
  428.1 14.2 %all_gather.10 = f32[2,2,256,128]{3,1,0,2:T(2,128)S(1)} all-gather(f32[2,2,32,128]{3,1,0,2:T(2,128)S(1)} %reduce_sum.146), channel_id=1, replica_groups=mesh['slab'=32,'coil'=8] {'coil'}, dimensions={2}, use_global_device_ids=true | all-gather | bytes 589824 | tf_op jit(solution)/shard_map/all_gather | solution.py:123
  453.8 21.1 %all_to_all.164 = bf16[2,2,2,256,128]{4,1,2,0,3:T(2,128)(2,1)S(1)} all-to-all(bf16[2,2,2,256,128]{4,1,2,0,3:T(2,128)(2,1)} %copy.415), channel_id=1, replica_groups=mesh['slab'=32,'coil'=8] {'slab'}, dimensions={3} | all-to-all | bytes 1048576 | tf_op jit(solution)/shard_map/all_to_all | solution.py:99
  478.3 20.3 %all_to_all.165 = bf16[2,2,64,8,128]{4,1,3,0,2:T(2,128)(2,1)S(1)} all-to-all(bf16[2,2,64,8,128]{4,1,3,0,2:T(2,128)(2,1)S(1)} %copy.419), channel_id=1, replica_groups=mesh['slab'=32,'coil'=8] {'slab'}, dimensions={2} | all-to-all | bytes 1048576 | tf_op jit(solution)/shard_map/all_to_all | solution.py:108
  503.0 16.8 %all_to_all.166 = f32[2,2,256,128]{3,1,0,2:T(2,128)} all-to-all(f32[2,2,256,128]{3,1,0,2:T(2,128)} %copy.423), channel_id=1, replica_groups=mesh['slab'=32,'coil'=8] {'coil'}, dimensions={2} | all-to-all | bytes 1048576 | tf_op jit(solution)/shard_map/all_to_all | solution.py:117
  523.3 19.5 %all_to_all.167 = f32[256,1,2]{2,1,0:T(1,128)} all-to-all(f32[256,1,2]{2,1,0:T(1,128)S(1)} %broadcast_in_dim.15), channel_id=1, replica_groups=mesh['slab'=32,'coil'=8] {'slab','coil'}, dimensions={0} | all-to-all | bytes 4096 | tf_op jit(solution)/shard_map/all_to_all | solution.py:130
  548.7 19.5 %all_to_all.168 = f32[256,1,1]{2,1,0:T(1,128)} all-to-all(f32[256,1,1]{2,1,0:T(1,128)S(1)} %broadcast_in_dim.16), channel_id=1, replica_groups=mesh['slab'=32,'coil'=8] {'slab','coil'}, dimensions={0} | all-to-all | bytes 2048 | tf_op jit(solution)/shard_map/all_to_all | solution.py:130
  572.2 13.6 %all_gather.11 = f32[2,2,256,128]{3,1,0,2:T(2,128)S(1)} all-gather(f32[2,2,32,128]{3,1,0,2:T(2,128)S(1)} %multiply_add_fusion.4), channel_id=1, replica_groups=mesh['slab'=32,'coil'=8] {'coil'}, dimensions={2}, use_global_device_ids=true | all-gather | bytes 589824 | tf_op jit(solution)/shard_map/all_gather | solution.py:123
  597.4 21.0 %all_to_all.169 = bf16[2,2,2,256,128]{4,1,2,0,3:T(2,128)(2,1)S(1)} all-to-all(bf16[2,2,2,256,128]{4,1,2,0,3:T(2,128)(2,1)} %copy.428), channel_id=1, replica_groups=mesh['slab'=32,'coil'=8] {'slab'}, dimensions={3} | all-to-all | bytes 1048576 | tf_op jit(solution)/shard_map/all_to_all | solution.py:99
  621.8 20.3 %all_to_all.170 = bf16[2,2,64,8,128]{4,1,3,0,2:T(2,128)(2,1)S(1)} all-to-all(bf16[2,2,64,8,128]{4,1,3,0,2:T(2,128)(2,1)S(1)} %copy.432), channel_id=1, replica_groups=mesh['slab'=32,'coil'=8] {'slab'}, dimensions={2} | all-to-all | bytes 1048576 | tf_op jit(solution)/shard_map/all_to_all | solution.py:108
  644.0 15.2 %all_to_all.171 = f32[2,2,256,128]{3,1,0,2:T(2,128)S(1)} all-to-all(f32[2,2,256,128]{3,1,0,2:T(2,128)S(1)} %copy.436), channel_id=1, replica_groups=mesh['slab'=32,'coil'=8] {'coil'}, dimensions={2} | all-to-all | bytes 1048576 | tf_op jit(solution)/shard_map/all_to_all | solution.py:117
  661.4 6.5 all-to-all-start.11
  668.3 12.6 %all-to-all-done.11 = f32[256,1,1]{2,1,0:T(1,128)S(1)} async-done(((f32[256,1,1]{2,1,0:T(1,128)}), f32[256,1,1]{2,1,0:T(1,128)S(1)}, u32[]{:S(2)}, u32[]{:S(2)}) %all-to-all-start.11) | async-done | bytes 1056 | tf_op jit(solution)/shard_map/all_to_all | solution.py:130
  (206 shorter events, 209.2 us)
Async XLA Ops:
  0.6 366.3 %copy-start = (f32[2,2,64,8,128]{4,3,2,1,0:T(8,128)S(1)}, f32[2,2,64,8,128]{4,3,2,1,0:T(8,128)}, u32[]{:S(2)}) copy-start(f32[2,2,64,8,128]{4,3,2,1,0:T(8,128)} %param.16) | copy-start | bytes 3145732
  1.6 5.9 collective-permute-start
  5.5 4.5 collective-permute-start.1
  10.0 8.1 %collective-permute-start.2 = (bf16[2,4,1,128]{3,2,1,0:T(2,128)(2,1)S(1)}, bf16[2,4,1,128]{3,2,1,0:T(2,128)(2,1)S(1)}, u32[]{:S(2)}, u32[]{:S(2)}) collective-permute-start(bf16[2,4,1,128]{3,2,1,0:T(2,128)(2,1)S(1)} %get-tuple-element.62), channel_id=1, source_target_pairs={{0,1},{1,2},{2,3},{3,4},{4,5},{5,6},{6,7},{8,9},{9,10},{10,11},{11... | collective-permute-start | bytes 6152 | tf_op jit(solution)/shard_map/ppermute | solution.py:22
  15.2 4.9 collective-permute-start.3
  36.8 10.5 %collective-permute-start.4 = (bf16[32,1,32,128]{3,2,1,0:T(8,128)(2,1)S(1)}, bf16[32,1,32,128]{3,2,1,0:T(8,128)(2,1)}, u32[]{:S(2)}, u32[]{:S(2)}) collective-permute-start(bf16[32,1,32,128]{3,2,1,0:T(8,128)(2,1)S(1)} %copy.380), channel_id=1, source_target_pairs={{0,8},{8,16},{16,24},{24,32},{32,40},{40,48},{48,56},{56,64},{64,7... | collective-permute-start | bytes 786440 | tf_op jit(solution)/shard_map/ppermute | solution.py:22
  44.2 9.1 %collective-permute-start.5 = (bf16[32,1,32,128]{3,2,1,0:T(8,128)(2,1)}, bf16[32,1,32,128]{3,2,1,0:T(8,128)(2,1)}, u32[]{:S(2)}, u32[]{:S(2)}) collective-permute-start(bf16[32,1,32,128]{3,2,1,0:T(8,128)(2,1)} %copy.381), channel_id=1, source_target_pairs={{8,0},{16,8},{24,16},{32,24},{40,32},{48,40},{56,48},{64,56},{72,6... | collective-permute-start | bytes 786440 | tf_op jit(solution)/shard_map/ppermute | solution.py:24
  58.9 7.7 %collective-permute-start.6 = (bf16[32,4,1,128]{0,2,3,1:T(2,128)(2,1)S(1)}, bf16[32,4,1,128]{0,2,3,1:T(2,128)(2,1)S(1)}, u32[]{:S(2)}, u32[]{:S(2)}) collective-permute-start(bf16[32,4,1,128]{0,2,3,1:T(2,128)(2,1)S(1)} %get-tuple-element.28), channel_id=1, source_target_pairs={{0,1},{1,2},{2,3},{3,4},{4,5},{5,6},{6,7},{8,9},{9,10},{10,11},{11... | collective-permute-start | bytes 98312 | tf_op jit(solution)/shard_map/ppermute | solution.py:22
  63.0 7.7 %collective-permute-start.7 = (bf16[32,4,1,128]{0,2,3,1:T(2,128)(2,1)S(1)}, bf16[32,4,1,128]{0,2,3,1:T(2,128)(2,1)S(1)}, u32[]{:S(2)}, u32[]{:S(2)}) collective-permute-start(bf16[32,4,1,128]{0,2,3,1:T(2,128)(2,1)S(1)} %get-tuple-element.29), channel_id=1, source_target_pairs={{1,0},{2,1},{3,2},{4,3},{5,4},{6,5},{7,6},{9,8},{10,9},{11,10},{12... | collective-permute-start | bytes 98312 | tf_op jit(solution)/shard_map/ppermute | solution.py:24
  115.4 11.5 %collective-permute-start.8 = (bf16[32,1,32,128]{3,2,1,0:T(8,128)(2,1)}, bf16[32,1,32,128]{3,2,1,0:T(8,128)(2,1)}, u32[]{:S(2)}, u32[]{:S(2)}) collective-permute-start(bf16[32,1,32,128]{3,2,1,0:T(8,128)(2,1)} %copy.388), channel_id=1, source_target_pairs={{0,8},{8,16},{16,24},{24,32},{32,40},{40,48},{48,56},{56,64},{64,7... | collective-permute-start | bytes 786440 | tf_op jit(solution)/shard_map/ppermute | solution.py:22
  123.2 7.6 %collective-permute-start.9 = (bf16[32,1,32,128]{3,2,1,0:T(8,128)(2,1)}, bf16[32,1,32,128]{3,2,1,0:T(8,128)(2,1)}, u32[]{:S(2)}, u32[]{:S(2)}) collective-permute-start(bf16[32,1,32,128]{3,2,1,0:T(8,128)(2,1)} %copy.389), channel_id=1, source_target_pairs={{8,0},{16,8},{24,16},{32,24},{40,32},{48,40},{56,48},{64,56},{72,6... | collective-permute-start | bytes 786440 | tf_op jit(solution)/shard_map/ppermute | solution.py:24
  137.0 12.9 %collective-permute-start.10 = (bf16[32,4,1,128]{0,2,3,1:T(2,128)(2,1)}, bf16[32,4,1,128]{0,2,3,1:T(2,128)(2,1)}, u32[]{:S(2)}, u32[]{:S(2)}) collective-permute-start(bf16[32,4,1,128]{0,2,3,1:T(2,128)(2,1)} %get-tuple-element.26), channel_id=1, source_target_pairs={{0,1},{1,2},{2,3},{3,4},{4,5},{5,6},{6,7},{8,9},{9,10},{10,11},{11... | collective-permute-start | bytes 98312 | tf_op jit(solution)/shard_map/ppermute | solution.py:22
  142.1 8.0 %collective-permute-start.11 = (bf16[32,4,1,128]{0,2,3,1:T(2,128)(2,1)}, bf16[32,4,1,128]{0,2,3,1:T(2,128)(2,1)}, u32[]{:S(2)}, u32[]{:S(2)}) collective-permute-start(bf16[32,4,1,128]{0,2,3,1:T(2,128)(2,1)} %get-tuple-element.27), channel_id=1, source_target_pairs={{1,0},{2,1},{3,2},{4,3},{5,4},{6,5},{7,6},{9,8},{10,9},{11,10},{12... | collective-permute-start | bytes 98312 | tf_op jit(solution)/shard_map/ppermute | solution.py:24
  319.3 24.9 %copy-start.2 = (f32[2,1,2,256,128]{3,4,1,2,0:T(8,128)S(1)}, f32[2,1,2,256,128]{3,4,1,2,0:T(8,128)}, u32[]{:S(2)}) copy-start(f32[2,1,2,256,128]{3,4,1,2,0:T(8,128)} %copy.490) | copy-start | bytes 1572868
  319.3 24.9 %copy-start.3 = (f32[2,1,2,256,128]{3,4,1,2,0:T(8,128)S(1)}, f32[2,1,2,256,128]{3,4,1,2,0:T(8,128)}, u32[]{:S(2)}) copy-start(f32[2,1,2,256,128]{3,4,1,2,0:T(8,128)} %copy.492) | copy-start | bytes 1572868
  319.3 26.1 %copy-start.8 = (f32[1,256,2,256]{3,1,2,0:T(8,128)S(1)}, f32[1,256,2,256]{3,1,2,0:T(8,128)}, u32[]{:S(2)}) copy-start(f32[1,256,2,256]{3,1,2,0:T(8,128)} %get-tuple-element.46) | copy-start | bytes 1572868
  319.3 26.1 %copy-start.9 = (f32[1,256,2,256]{3,1,2,0:T(8,128)S(1)}, f32[1,256,2,256]{3,1,2,0:T(8,128)}, u32[]{:S(2)}) copy-start(f32[1,256,2,256]{3,1,2,0:T(8,128)} %get-tuple-element.55) | copy-start | bytes 1572868
  325.5 24.5 %copy-start.22 = (f32[2,2,32,128]{3,1,0,2:T(2,128)}, f32[2,2,32,128]{3,1,0,2:T(2,128)S(1)}, u32[]{:S(2)}) copy-start(f32[2,2,32,128]{3,1,0,2:T(2,128)S(1)} %fusion.74) | copy-start | bytes 196612
  340.6 24.1 %copy-start.24 = (s32[64,8]{0,1:T(8,128)S(1)}, s32[64,8]{0,1:T(8,128)}, u32[]{:S(2)}) copy-start(s32[64,8]{0,1:T(8,128)} %param.17) | copy-start | bytes 6148
  350.0 31.4 %all-to-all-start = ((bf16[2,2,2,256,128]{4,1,2,0,3:T(2,128)(2,1)}), bf16[2,2,2,256,128]{4,1,2,0,3:T(2,128)(2,1)S(1)}, u32[]{:S(2)}, u32[]{:S(2)}) async-start(bf16[2,2,2,256,128]{4,1,2,0,3:T(2,128)(2,1)} %copy.404), calls=%async_computation | async-start | bytes 1048576 | tf_op jit(solution)/shard_map/all_to_all | solution.py:99
  366.9 108.2 %copy-start.14 = (f32[1,64,2,64]{3,1,2,0:T(8,128)}, f32[1,64,2,64]{3,1,2,0:T(8,128)S(1)}, u32[]{:S(2)}) copy-start(f32[1,64,2,64]{3,1,2,0:T(8,128)S(1)} %get-tuple-element.57) | copy-start | bytes 98308
  521.0 49.0 %copy-start.10 = (f32[2,2,32,128]{3,1,0,2:T(2,128)}, f32[2,2,32,128]{3,1,0,2:T(2,128)S(1)}, u32[]{:S(2)}) copy-start(f32[2,2,32,128]{3,1,0,2:T(2,128)S(1)} %reduce_sum.150) | copy-start | bytes 196612
  643.4 39.7 %copy-start.23 = (f32[2,2,32,128]{3,1,0,2:T(2,128)S(1)}, f32[2,2,32,128]{3,1,0,2:T(2,128)}, u32[]{:S(2)}) copy-start(f32[2,2,32,128]{3,1,0,2:T(2,128)} %copy-done.22) | copy-start | bytes 196612
  661.4 19.5 %all-to-all-start.11 = ((f32[256,1,1]{2,1,0:T(1,128)}), f32[256,1,1]{2,1,0:T(1,128)S(1)}, u32[]{:S(2)}, u32[]{:S(2)}) async-start(f32[256,1,1]{2,1,0:T(1,128)} %broadcast_in_dim.17), calls=%async_computation.11 | async-start | bytes 262144 | tf_op jit(solution)/shard_map/all_to_all | solution.py:130
  (20 other events, 290.6 us)
where the time goes:
time: 697 us; the launch traced here: 685 us
  blocking collectives  233 us (33%)
  matrix products  181 us (26%)
  local copies, waits for them, and re-layouts  123 us (18%)
  starting transfers between devices  57.9 us (8%)
  other arithmetic  46.4 us (7%)
  waiting for transfers between devices  36.7 us (5%)
    conv_general_dilated x3, matrix products, conv_layer(): lax.conv_general_dilated(padded[None], kernel, (1, 1, 1), ((0, 0), (0, 0)...  156 us
    all_to_all x3, blocking collectives, coil_term(): lax.all_to_all(back.astype(jnp.bfloat16), 'slab', split_axis=2, concat_ax...  60.9 us
    all_to_all x3, blocking collectives, combine_coils(): lax.all_to_all(partial_value, 'coil', split_axis=2, concat_axis=0, tiled=...  48.8 us
    all_to_all x2, blocking collectives, coil_term(): lax.all_to_all(spectrum.astype(jnp.bfloat16), 'slab', split_axis=3, conca...  42.1 us
    all_gather x3, blocking collectives, gather_rows(): return lax.all_gather(value, 'coil', axis=2, tiled=True)  42 us
    all_to_all x2, blocking collectives, global_sums(): lax.all_to_all(spread, axes, split_axis=0, concat_axis=0, tiled=True)  39 us
    ppermute x6, starting transfers between devices, extended(): lax.ppermute(tail, axis, [(i, (i + 1) % count) for i in range(ends)])  27 us
    conv_general_dilated x9, local copies, waits for them, and re-layouts, conv_layer(): lax.conv_general_dilated(padded[None], kernel, (1, 1, 1), ((0, 0), (0, 0)...  26 us
  transfers between devices with their start and end apart: 14, of which 8 were waited for; matrix products, arithmetic and copies ran while one was open for 4% of the time, Pallas kernels for 0%

commit v1 on v0

--- a/solution.py
+++ b/solution.py
@@ -120,7 +120,9 @@
 
 
 def gather_rows(value):
-    return lax.all_gather(value, "coil", axis=2, tiled=True)
+    return jnp.concatenate(
+        lax.all_to_all(jnp.stack([value] * lax.axis_size("coil")), "coil", 0, 0), axis=2
+    )
 
 
 def global_sums(values):

time: 697 us -> 689 us (0.989)
  blocking collectives: 233 us -> 217 us
  waiting for transfers between devices: 36.7 us -> 50.6 us
    all_gather x3 -> x0, blocking collectives: 42 us -> none  [gather_rows(): return lax.all_gather(value, 'coil', axis=2, tiled=True)]
    all_to_all x0 -> x2, blocking collectives: none -> 25.6 us  [gather_rows(): lax.all_to_all(jnp.stack([value] * lax.axis_size('coil')), 'coil', 0, 0)]
    ppermute x6, waiting for transfers between devices: 11.5 us -> 20.1 us  [extended(): lax.ppermute(head, axis, [((i + 1) % count, i) for i in range(ends)])]
    unnamed x69 -> x53, local copies, waits for them, and re-layouts: 23.1 us -> 19 us
  transfers between devices with their start and end apart: 14 -> 15, of which waited for: 8 -> 11; matrix products, arithmetic and copies ran while one was open for 4% -> 4% of each run, Pallas kernels for 0% -> 0%
where the time goes in v1:
time: 689 us; the launch traced here: 678 us
  blocking collectives  217 us (31%)
  matrix products  182 us (26%)
  local copies, waits for them, and re-layouts  117 us (17%)
  starting transfers between devices  61.9 us (9%)
  waiting for transfers between devices  50.6 us (7%)
  other arithmetic  42.6 us (6%)
    conv_general_dilated x3, matrix products, conv_layer(): lax.conv_general_dilated(padded[None], kernel, (1, 1, 1), ((0, 0), (0, 0)...  155 us
    all_to_all x3, blocking collectives, coil_term(): lax.all_to_all(back.astype(jnp.bfloat16), 'slab', split_axis=2, concat_ax...  63.5 us
    all_to_all x3, blocking collectives, combine_coils(): lax.all_to_all(partial_value, 'coil', split_axis=2, concat_axis=0, tiled=...  49.4 us
    all_to_all x2, blocking collectives, coil_term(): lax.all_to_all(spectrum.astype(jnp.bfloat16), 'slab', split_axis=3, conca...  39.3 us
    all_to_all x2, blocking collectives, global_sums(): lax.all_to_all(spread, axes, split_axis=0, concat_axis=0, tiled=True)  39.1 us
    ppermute x6, starting transfers between devices, extended(): lax.ppermute(tail, axis, [(i, (i + 1) % count) for i in range(ends)])  27 us
    all_to_all x2, blocking collectives, gather_rows(): lax.all_to_all(jnp.stack([value] * lax.axis_size('coil')), 'coil', 0, 0)  25.6 us
    conv_general_dilated x9, local copies, waits for them, and re-layouts, conv_layer(): lax.conv_general_dilated(padded[None], kernel, (1, 1, 1), ((0, 0), (0, 0)...  24.2 us
  transfers between devices with their start and end apart: 15, of which 11 were waited for; matrix products, arithmetic and copies ran while one was open for 4% of the time, Pallas kernels for 0%

profile of v1, /device:TPU:1, one launch (start us, length us, event | category | flops | bytes accessed | tf_op | source)
XLA Modules:
  0.0 677.8 jit_solution(5427869748281032894)
XLA Ops:
  22.7 7.8 %broadcast_select_fusion.1 = f32[2,32,8,17,32]{4,2,3,1,0:T(8,128)S(1)} fusion(pred[8,17]{0,1:T(8,128)(4,1)} %constant.113, bf16[3,3,3,32,2]{3,4,2,1,0:T(2,128)(2,1)} %param.11, bf16[2,4,34,1,7,2]{4,0,5,2,1,3:T(2,128)(2,1)S(1)} %slice.161, bf16[2,4,34,1,8,17]{4,0,5,2,1,3:T(2,128)(2,1)S(1)} %copy.408), kind=kOutput, calls=%fused_computation.23 | convolution fusion | flops 30607616 | bytes 1199304 | tf_op jit(solution)/shard_map/conv_general_dilated | solution.py:47
  75.3 8.1 %copy.533 = bf16[32,4,34,1,128]{2,0,4,1,3:T(8,128)(2,1)} copy(bf16[32,4,34,1,128]{0,2,4,1,3:T(8,128)(2,1)} %maximum_bitcast_fusion) | data formatting | bytes 2228224
  88.6 8.7 %copy.416 = bf16[32,4,34,1,8,17]{0,4,5,2,1,3:T(8,128)(2,1)} copy(bf16[32,4,34,1,8,17]{2,0,5,4,1,3:T(8,128)(2,1)} %bitcast.331) | data formatting | bytes 2367488 | tf_op jit(solution)/shard_map/conv_general_dilated | solution.py:47
  98.6 8.6 %broadcast_select_fusion = f32[2,32,8,17,32]{4,2,3,1,0:T(8,128)S(1)} fusion(pred[8,17]{0,1:T(8,128)(4,1)S(1)} %copy-done.17, bf16[3,3,3,32,32]{4,3,2,1,0:T(8,128)(2,1)S(1)} %copy-done.18, bf16[32,4,34,1,7,2]{0,4,5,2,1,3:T(8,128)(2,1)S(1)} %slice.165, bf16[32,4,34,1,8,17]{0,4,5,2,1,3:T(8,128)(2,1)} %copy.416), kind=kOutput, calls=%fused_computation.22 | convolution fusion | flops 485543936 | bytes 2475144 | tf_op jit(solution)/shard_map/conv_general_dilated | solution.py:47
  149.3 6.3 maximum_bitcast_fusion.1
  155.6 8.1 %copy.534 = bf16[32,4,34,1,128]{2,0,4,1,3:T(8,128)(2,1)} copy(bf16[32,4,34,1,128]{0,2,4,1,3:T(8,128)(2,1)} %maximum_bitcast_fusion.1) | data formatting | bytes 2228224
  168.8 8.7 %copy.424 = bf16[32,4,34,1,8,17]{0,4,5,2,1,3:T(8,128)(2,1)} copy(bf16[32,4,34,1,8,17]{2,0,5,4,1,3:T(8,128)(2,1)} %bitcast.330) | data formatting | bytes 2367488 | tf_op jit(solution)/shard_map/conv_general_dilated | solution.py:47
  178.7 138.9 %fusion.11 = f32[2,32,8,17,2]{2,4,3,1,0:T(2,128)S(1)} fusion(bf16[3,3,3,2,32]{4,3,2,1,0:T(2,128)(2,1)S(1)} %copy-done.19, bf16[32,4,34,1,7,2]{0,4,5,2,1,3:T(8,128)(2,1)S(1)} %slice.169, bf16[32,4,34,1,8,17]{0,4,5,2,1,3:T(8,128)(2,1)} %copy.424), kind=kOutput, calls=%fused_computation.11 | convolution fusion | flops 34050048 | bytes 1378688 | tf_op jit(solution)/shard_map/conv_general_dilated | solution.py:47
  345.5 14.8 %all-to-all-start.1 = ((bf16[2,2,2,256,128]{4,1,2,0,3:T(2,128)(2,1)}), bf16[2,2,2,256,128]{4,1,2,0,3:T(2,128)(2,1)}, u32[]{:S(2)}, u32[]{:S(2)}) async-start(bf16[2,2,2,256,128]{4,1,2,0,3:T(2,128)(2,1)} %copy.436), calls=%async_computation.1 | async-start | bytes 1048576 | tf_op jit(solution)/shard_map/all_to_all | solution.py:99
  364.6 11.2 %all-to-all-done.1 = bf16[2,2,2,256,128]{4,1,2,0,3:T(2,128)(2,1)} async-done(((bf16[2,2,2,256,128]{4,1,2,0,3:T(2,128)(2,1)}), bf16[2,2,2,256,128]{4,1,2,0,3:T(2,128)(2,1)}, u32[]{:S(2)}, u32[]{:S(2)}) %all-to-all-start.1) | async-done | bytes 524320 | tf_op jit(solution)/shard_map/all_to_all | solution.py:99
  380.6 21.4 %all_to_all.177 = bf16[2,2,64,8,128]{4,1,3,0,2:T(2,128)(2,1)S(1)} all-to-all(bf16[2,2,64,8,128]{4,1,3,0,2:T(2,128)(2,1)S(1)} %copy.440), channel_id=1, replica_groups=mesh['slab'=32,'coil'=8] {'slab'}, dimensions={2} | all-to-all | bytes 1048576 | tf_op jit(solution)/shard_map/all_to_all | solution.py:108
  406.4 17.0 %all_to_all.178 = f32[2,2,256,128]{3,1,0,2:T(2,128)} all-to-all(f32[2,2,256,128]{3,1,0,2:T(2,128)} %copy.444), channel_id=1, replica_groups=mesh['slab'=32,'coil'=8] {'coil'}, dimensions={2} | all-to-all | bytes 1048576 | tf_op jit(solution)/shard_map/all_to_all | solution.py:117
  424.7 12.8 %all_to_all.179 = f32[8,2,2,32,128]{4,3,2,1,0:T(8,128)S(1)} all-to-all(f32[8,2,2,32,128]{4,3,2,1,0:T(8,128)S(1)} %stack.210), channel_id=1, replica_groups=mesh['slab'=32,'coil'=8] {'coil'}, dimensions={0} | all-to-all | bytes 1048576 | tf_op jit(solution)/shard_map/all_to_all | solution.py:124
  448.9 19.7 %all_to_all.180 = bf16[2,2,2,256,128]{4,1,2,0,3:T(2,128)(2,1)S(1)} all-to-all(bf16[2,2,2,256,128]{4,1,2,0,3:T(2,128)(2,1)} %copy.449), channel_id=1, replica_groups=mesh['slab'=32,'coil'=8] {'slab'}, dimensions={3} | all-to-all | bytes 1048576 | tf_op jit(solution)/shard_map/all_to_all | solution.py:99
  471.9 21.2 %all_to_all.181 = bf16[2,2,64,8,128]{4,1,3,0,2:T(2,128)(2,1)S(1)} all-to-all(bf16[2,2,64,8,128]{4,1,3,0,2:T(2,128)(2,1)S(1)} %copy.453), channel_id=1, replica_groups=mesh['slab'=32,'coil'=8] {'slab'}, dimensions={2} | all-to-all | bytes 1048576 | tf_op jit(solution)/shard_map/all_to_all | solution.py:108
  497.6 17.0 %all_to_all.182 = f32[2,2,256,128]{3,1,0,2:T(2,128)} all-to-all(f32[2,2,256,128]{3,1,0,2:T(2,128)} %copy.457), channel_id=1, replica_groups=mesh['slab'=32,'coil'=8] {'coil'}, dimensions={2} | all-to-all | bytes 1048576 | tf_op jit(solution)/shard_map/all_to_all | solution.py:117
  517.9 19.9 %all_to_all.183 = f32[256,1,2]{2,1,0:T(1,128)} all-to-all(f32[256,1,2]{2,1,0:T(1,128)S(1)} %broadcast_in_dim.15), channel_id=1, replica_groups=mesh['slab'=32,'coil'=8] {'slab','coil'}, dimensions={0} | all-to-all | bytes 4096 | tf_op jit(solution)/shard_map/all_to_all | solution.py:132
  543.5 19.2 %all_to_all.184 = f32[256,1,1]{2,1,0:T(1,128)} all-to-all(f32[256,1,1]{2,1,0:T(1,128)S(1)} %broadcast_in_dim.16), channel_id=1, replica_groups=mesh['slab'=32,'coil'=8] {'slab','coil'}, dimensions={0} | all-to-all | bytes 2048 | tf_op jit(solution)/shard_map/all_to_all | solution.py:132
  566.9 12.8 %all_to_all.185 = f32[8,2,2,32,128]{4,3,2,1,0:T(8,128)S(1)} all-to-all(f32[8,2,2,32,128]{4,3,2,1,0:T(8,128)S(1)} %stack.217), channel_id=1, replica_groups=mesh['slab'=32,'coil'=8] {'coil'}, dimensions={0} | all-to-all | bytes 1048576 | tf_op jit(solution)/shard_map/all_to_all | solution.py:124
  591.1 19.6 %all_to_all.186 = bf16[2,2,2,256,128]{4,1,2,0,3:T(2,128)(2,1)S(1)} all-to-all(bf16[2,2,2,256,128]{4,1,2,0,3:T(2,128)(2,1)} %copy.464), channel_id=1, replica_groups=mesh['slab'=32,'coil'=8] {'slab'}, dimensions={3} | all-to-all | bytes 1048576 | tf_op jit(solution)/shard_map/all_to_all | solution.py:99
  614.1 20.9 %all_to_all.187 = bf16[2,2,64,8,128]{4,1,3,0,2:T(2,128)(2,1)S(1)} all-to-all(bf16[2,2,64,8,128]{4,1,3,0,2:T(2,128)(2,1)S(1)} %copy.468), channel_id=1, replica_groups=mesh['slab'=32,'coil'=8] {'slab'}, dimensions={2} | all-to-all | bytes 1048576 | tf_op jit(solution)/shard_map/all_to_all | solution.py:108
  636.8 15.4 %all_to_all.188 = f32[2,2,256,128]{3,1,0,2:T(2,128)S(1)} all-to-all(f32[2,2,256,128]{3,1,0,2:T(2,128)S(1)} %copy.472), channel_id=1, replica_groups=mesh['slab'=32,'coil'=8] {'coil'}, dimensions={2} | all-to-all | bytes 1048576 | tf_op jit(solution)/shard_map/all_to_all | solution.py:117
  654.4 6.4 all-to-all-start.14
  661.1 12.6 %all-to-all-done.14 = f32[256,1,1]{2,1,0:T(1,128)S(1)} async-done(((f32[256,1,1]{2,1,0:T(1,128)}), f32[256,1,1]{2,1,0:T(1,128)S(1)}, u32[]{:S(2)}, u32[]{:S(2)}) %all-to-all-start.14) | async-done | bytes 1056 | tf_op jit(solution)/shard_map/all_to_all | solution.py:132
  (200 shorter events, 213.8 us)
Async XLA Ops:
  0.6 361.9 %copy-start = (f32[2,2,64,8,128]{4,3,2,1,0:T(8,128)S(1)}, f32[2,2,64,8,128]{4,3,2,1,0:T(8,128)}, u32[]{:S(2)}) copy-start(f32[2,2,64,8,128]{4,3,2,1,0:T(8,128)} %param.16) | copy-start | bytes 3145732
  1.6 5.9 collective-permute-start
  5.5 4.5 collective-permute-start.1
  10.0 8.1 %collective-permute-start.2 = (bf16[2,4,1,128]{3,2,1,0:T(2,128)(2,1)S(1)}, bf16[2,4,1,128]{3,2,1,0:T(2,128)(2,1)S(1)}, u32[]{:S(2)}, u32[]{:S(2)}) collective-permute-start(bf16[2,4,1,128]{3,2,1,0:T(2,128)(2,1)S(1)} %get-tuple-element.62), channel_id=1, source_target_pairs={{0,1},{1,2},{2,3},{3,4},{4,5},{5,6},{6,7},{8,9},{9,10},{10,11},{11... | collective-permute-start | bytes 6152 | tf_op jit(solution)/shard_map/ppermute | solution.py:22
  15.2 4.9 collective-permute-start.3
  36.8 8.8 %collective-permute-start.4 = (bf16[32,1,32,128]{3,2,1,0:T(8,128)(2,1)S(1)}, bf16[32,1,32,128]{3,2,1,0:T(8,128)(2,1)}, u32[]{:S(2)}, u32[]{:S(2)}) collective-permute-start(bf16[32,1,32,128]{3,2,1,0:T(8,128)(2,1)S(1)} %copy.410), channel_id=1, source_target_pairs={{0,8},{8,16},{16,24},{24,32},{32,40},{40,48},{48,56},{56,64},{64,7... | collective-permute-start | bytes 786440 | tf_op jit(solution)/shard_map/ppermute | solution.py:22
  44.3 9.1 %collective-permute-start.5 = (bf16[32,1,32,128]{3,2,1,0:T(8,128)(2,1)}, bf16[32,1,32,128]{3,2,1,0:T(8,128)(2,1)}, u32[]{:S(2)}, u32[]{:S(2)}) collective-permute-start(bf16[32,1,32,128]{3,2,1,0:T(8,128)(2,1)} %copy.411), channel_id=1, source_target_pairs={{8,0},{16,8},{24,16},{32,24},{40,32},{48,40},{56,48},{64,56},{72,6... | collective-permute-start | bytes 786440 | tf_op jit(solution)/shard_map/ppermute | solution.py:24
  58.9 7.4 %collective-permute-start.6 = (bf16[32,4,1,128]{0,2,3,1:T(2,128)(2,1)S(1)}, bf16[32,4,1,128]{0,2,3,1:T(2,128)(2,1)S(1)}, u32[]{:S(2)}, u32[]{:S(2)}) collective-permute-start(bf16[32,4,1,128]{0,2,3,1:T(2,128)(2,1)S(1)} %get-tuple-element.28), channel_id=1, source_target_pairs={{0,1},{1,2},{2,3},{3,4},{4,5},{5,6},{6,7},{8,9},{9,10},{10,11},{11... | collective-permute-start | bytes 98312 | tf_op jit(solution)/shard_map/ppermute | solution.py:22
  63.0 7.7 %collective-permute-start.7 = (bf16[32,4,1,128]{0,2,3,1:T(2,128)(2,1)S(1)}, bf16[32,4,1,128]{0,2,3,1:T(2,128)(2,1)S(1)}, u32[]{:S(2)}, u32[]{:S(2)}) collective-permute-start(bf16[32,4,1,128]{0,2,3,1:T(2,128)(2,1)S(1)} %get-tuple-element.29), channel_id=1, source_target_pairs={{1,0},{2,1},{3,2},{4,3},{5,4},{6,5},{7,6},{9,8},{10,9},{11,10},{12... | collective-permute-start | bytes 98312 | tf_op jit(solution)/shard_map/ppermute | solution.py:24
  114.8 9.1 %collective-permute-start.8 = (bf16[32,1,32,128]{3,2,1,0:T(8,128)(2,1)S(1)}, bf16[32,1,32,128]{3,2,1,0:T(8,128)(2,1)}, u32[]{:S(2)}, u32[]{:S(2)}) collective-permute-start(bf16[32,1,32,128]{3,2,1,0:T(8,128)(2,1)S(1)} %copy.418), channel_id=1, source_target_pairs={{0,8},{8,16},{16,24},{24,32},{32,40},{40,48},{48,56},{56,64},{64,7... | collective-permute-start | bytes 786440 | tf_op jit(solution)/shard_map/ppermute | solution.py:22
  122.6 7.4 %collective-permute-start.9 = (bf16[32,1,32,128]{3,2,1,0:T(8,128)(2,1)}, bf16[32,1,32,128]{3,2,1,0:T(8,128)(2,1)}, u32[]{:S(2)}, u32[]{:S(2)}) collective-permute-start(bf16[32,1,32,128]{3,2,1,0:T(8,128)(2,1)} %copy.419), channel_id=1, source_target_pairs={{8,0},{16,8},{24,16},{32,24},{40,32},{48,40},{56,48},{64,56},{72,6... | collective-permute-start | bytes 786440 | tf_op jit(solution)/shard_map/ppermute | solution.py:24
  136.2 8.7 %collective-permute-start.10 = (bf16[32,4,1,128]{0,2,3,1:T(2,128)(2,1)}, bf16[32,4,1,128]{0,2,3,1:T(2,128)(2,1)S(1)}, u32[]{:S(2)}, u32[]{:S(2)}) collective-permute-start(bf16[32,4,1,128]{0,2,3,1:T(2,128)(2,1)} %get-tuple-element.26), channel_id=1, source_target_pairs={{0,1},{1,2},{2,3},{3,4},{4,5},{5,6},{6,7},{8,9},{9,10},{10,11},{11... | collective-permute-start | bytes 98312 | tf_op jit(solution)/shard_map/ppermute | solution.py:22
  141.3 8.0 %collective-permute-start.11 = (bf16[32,4,1,128]{0,2,3,1:T(2,128)(2,1)}, bf16[32,4,1,128]{0,2,3,1:T(2,128)(2,1)}, u32[]{:S(2)}, u32[]{:S(2)}) collective-permute-start(bf16[32,4,1,128]{0,2,3,1:T(2,128)(2,1)} %get-tuple-element.27), channel_id=1, source_target_pairs={{1,0},{2,1},{3,2},{4,3},{5,4},{6,5},{7,6},{9,8},{10,9},{11,10},{12... | collective-permute-start | bytes 98312 | tf_op jit(solution)/shard_map/ppermute | solution.py:24
  178.7 139.9 %copy-start.15 = (f32[2,2,32,128]{3,2,1,0:T(8,128)S(1)}, f32[2,2,32,128]{3,2,1,0:T(8,128)}, u32[]{:S(2)}) copy-start(f32[2,2,32,128]{3,2,1,0:T(8,128)} %param.9) | copy-start | bytes 196612
  320.1 12.9 %all-to-all-start = ((f32[8,2,2,32,128]{4,3,2,1,0:T(8,128)}), f32[8,2,2,32,128]{4,3,2,1,0:T(8,128)}, u32[]{:S(2)}, u32[]{:S(2)}) async-start(f32[8,2,2,32,128]{4,3,2,1,0:T(8,128)} %stack.91), calls=%async_computation | async-start | bytes 1048576 | tf_op jit(solution)/shard_map/all_to_all | solution.py:124
  334.9 25.4 %copy-start.16 = (s32[64,8]{0,1:T(8,128)S(1)}, s32[64,8]{0,1:T(8,128)}, u32[]{:S(2)}) copy-start(s32[64,8]{0,1:T(8,128)} %param.17) | copy-start | bytes 6148
  345.5 30.2 %all-to-all-start.1 = ((bf16[2,2,2,256,128]{4,1,2,0,3:T(2,128)(2,1)}), bf16[2,2,2,256,128]{4,1,2,0,3:T(2,128)(2,1)}, u32[]{:S(2)}, u32[]{:S(2)}) async-start(bf16[2,2,2,256,128]{4,1,2,0,3:T(2,128)(2,1)} %copy.436), calls=%async_computation.1 | async-start | bytes 1048576 | tf_op jit(solution)/shard_map/all_to_all | solution.py:99
  362.5 106.3 %copy-start.5 = (f32[1,64,2,64]{3,1,2,0:T(8,128)}, f32[1,64,2,64]{3,1,2,0:T(8,128)S(1)}, u32[]{:S(2)}) copy-start(f32[1,64,2,64]{3,1,2,0:T(8,128)S(1)} %get-tuple-element.57) | copy-start | bytes 98308
  448.9 21.4 %copy-start.8 = (f32[1,64,2,64]{3,1,2,0:T(8,128)S(1)}, f32[1,64,2,64]{3,1,2,0:T(8,128)}, u32[]{:S(2)}) copy-start(f32[1,64,2,64]{3,1,2,0:T(8,128)} %get-tuple-element.56) | copy-start | bytes 98308
  448.9 21.4 %copy-start.11 = (f32[1,64,2,64]{3,1,2,0:T(8,128)S(1)}, f32[1,64,2,64]{3,1,2,0:T(8,128)}, u32[]{:S(2)}) copy-start(f32[1,64,2,64]{3,1,2,0:T(8,128)} %get-tuple-element.65) | copy-start | bytes 98308
  515.8 48.8 %copy-start.4 = (f32[2,2,32,128]{3,1,0,2:T(2,128)}, f32[2,2,32,128]{3,1,0,2:T(2,128)S(1)}, u32[]{:S(2)}) copy-start(f32[2,2,32,128]{3,1,0,2:T(2,128)S(1)} %reduce_sum.150) | copy-start | bytes 196612
  591.1 21.2 %copy-start.12 = (f32[1,64,2,64]{3,1,2,0:T(8,128)S(1)}, f32[1,64,2,64]{3,1,2,0:T(8,128)}, u32[]{:S(2)}) copy-start(f32[1,64,2,64]{3,1,2,0:T(8,128)} %get-tuple-element.65) | copy-start | bytes 98308
  636.2 39.7 %copy-start.14 = (f32[2,2,32,128]{3,1,0,2:T(2,128)S(1)}, f32[2,2,32,128]{3,1,0,2:T(2,128)}, u32[]{:S(2)}) copy-start(f32[2,2,32,128]{3,1,0,2:T(2,128)} %copy-done.13) | copy-start | bytes 196612
  654.4 19.4 %all-to-all-start.14 = ((f32[256,1,1]{2,1,0:T(1,128)}), f32[256,1,1]{2,1,0:T(1,128)S(1)}, u32[]{:S(2)}, u32[]{:S(2)}) async-start(f32[256,1,1]{2,1,0:T(1,128)} %broadcast_in_dim.17), calls=%async_computation.14 | async-start | bytes 262144 | tf_op jit(solution)/shard_map/all_to_all | solution.py:132
  (13 other events, 134.6 us)
